TPU v7x, 256 devices: a whole 4x4x8 slice. The times are simulated.
256 devices in a mesh: row: 8 (over z), col: 32 (over y, x, core).
Axes of the slice: x: 4, y: 4, z: 8, core: 2. Of those that a mesh axis runs over, the one named last changes fastest.
Arguments:
- hidden_in: bfloat16 [3072, 2, 7168], P('row', None, 'col'), may hold values from -16 to 16
- final_gain: float32 [2, 7168], P(None, 'col'), may hold values from 0.25 to 1.75
- unembed: bfloat16 [7168, 32768], P('row', 'col'), may hold values from -2 to 2
- lengths: int32 [16], replicated, may hold values from 1 to 768, 3072 in all
- targets: int32 [3072], P('row'), may hold values from 0 to 32767
- owner: int32 [16], replicated, may hold values from 0 to 31
Outputs:
- owner_table: float32 [32, 3, 16], P('col')
Inputs may be any that keep to these rules, and one draw needn't show every extreme that they name: The lengths sum to 3072; the longest is exactly 768.
All inputs are finite; a program needn't handle non-finite values.
Results may differ from a plain program's by a relative error of at most 0.00056.
Values may be sent and summed in bfloat16 or wider, within the bound.
No kernel may reach another device: no remote copies, remote signals or barrier semaphores. Data moves between devices by JAX's collectives and lax.ppermute only.
A program may use at most 128 MiB of HBM per device.

v0:
```python
import jax
import jax.numpy as jnp
from jax import lax
from jax.sharding import PartitionSpec as P

D = 7168
EPS = 1e-05


def per_device(hidden_in, final_gain, unembed, lengths, targets, owner):
    tok_rows = hidden_in.shape[0]
    vocab_cols = unembed.shape[1]
    col_index = lax.axis_index("col")
    row_index = lax.axis_index("row")
    full_unembed = lax.all_gather(unembed, "row", axis=0, tiled=True)
    full_hidden = lax.all_gather(hidden_in, "col", axis=2, tiled=True)
    full_gain = lax.all_gather(final_gain, "col", axis=1, tiled=True)
    stream = full_hidden.astype(jnp.float32)
    mean_square = jnp.sum(stream * stream, axis=2) / D
    features = (stream * lax.rsqrt(mean_square[:, :, None] + EPS) * full_gain[None, :, :]).astype(
        jnp.bfloat16
    )
    logits = jnp.einsum("tmd,dv->tmv", features, full_unembed, preferred_element_type=jnp.float32)
    row_max = jnp.max(logits, axis=2)
    exp_total = jnp.sum(jnp.exp(logits - row_max[:, :, None]), axis=2)
    vocab_ids = col_index * vocab_cols + jnp.arange(vocab_cols, dtype=jnp.int32)
    picked = jnp.sum(
        jnp.where(targets[:, None, None] == vocab_ids[None, None, :], logits, 0.0), axis=2
    )
    parts = lax.all_gather(jnp.stack([row_max, exp_total, picked]), "col")
    max_logit = jnp.max(parts[:, 0], axis=0)
    exp_total = jnp.sum(parts[:, 1] * jnp.exp(parts[:, 0] - max_logit[None]), axis=0)
    picked = jnp.sum(parts[:, 2], axis=0)
    logp = picked - (max_logit + jnp.log(exp_total))
    log_ratio = logp[:, 0] - logp[:, 1]
    token_index = row_index * tok_rows + jnp.arange(tok_rows, dtype=jnp.int32)
    seq_ends = jnp.cumsum(lengths)
    segment = jnp.sum((seq_ends[None, :] <= token_index[:, None]).astype(jnp.int32), axis=1)
    member = segment[:, None] == jnp.arange(lengths.shape[0], dtype=jnp.int32)[None, :]
    ratio_sums = jnp.sum(jnp.where(member, log_ratio[:, None], 0.0), axis=0)
    squares = jnp.sum(jnp.where(member, (log_ratio * log_ratio)[:, None], 0.0), axis=0)
    ratio_max = jnp.max(jnp.where(member, log_ratio[:, None], -1e30), axis=0)
    stats = lax.all_gather(jnp.stack([ratio_sums, squares, ratio_max]), "row")
    seq_stats = jnp.stack(
        [jnp.sum(stats[:, 0], axis=0), jnp.sum(stats[:, 1], axis=0), jnp.max(stats[:, 2], axis=0)]
    )
    owned = owner == col_index
    return jnp.where(owned[None, :], seq_stats, 0.0)[None]


def solution(mesh):
    in_specs = (P("row", None, "col"), P(None, "col"), P("row", "col"), P(), P("row"), P())
    out_specs = P("col", None, None)
    return jax.shard_map(
        per_device, mesh=mesh, in_specs=in_specs, out_specs=out_specs, check_vma=False
    )
```

profile of v0, /device:TPU:32, one launch (start us, length us, event | category | flops | bytes accessed | tf_op | source)
XLA Modules:
  0.0 305.3 jit_solution(1823025273057362841)
XLA Ops:
  6.5 0.0 all-gather.7.cloned.1.call-start
  6.5 0.7 all-gather.7.cloned.1.call-update
  7.3 0.0 all-gather.9.cloned.1.call-start
  7.3 0.7 all-gather.9.cloned.1.call-update
  8.0 24.5 %all-gather.2 = f32[32,224,2]{1,2,0:T(2,128)S(1)} all-gather(f32[1,224,2]{1,2,0:T(2,128)} %bitcast.49), channel_id=1, replica_groups=mesh['row'=8,'col'=32] {'col'}, dimensions={0}, use_global_device_ids=true | all-gather | bytes 59136 | tf_op jit(solution)/shard_map/all_gather | solution.py:17
  32.6 0.1 reshape.144
  32.7 0.7 copy.21
  33.5 0.1 reduce.5
  33.6 0.1 convert_reduce_fusion
  33.7 0.7 broadcast_compare_fusion.1
  34.4 1.0 broadcast_compare_fusion
  35.3 41.2 %all-gather.7.cloned.1.call-done = bf16[384,2,7168]{0,2,1:T(8,128)(2,1)} async-done(((bf16[384,2,224]{0,2,1:T(8,128)(2,1)}), bf16[384,2,7168]{0,2,1:T(8,128)(2,1)}) %all-gather.7.cloned.1.call-update) | async-done | bytes 11010064 | tf_op jit(solution)/shard_map/all_gather | solution.py:16
  76.6 6.3 %fusion = f32[384,2]{0,1:T(2,128)S(1)} fusion(bf16[384,2,7168]{0,2,1:T(8,128)(2,1)} %all-gather.7.cloned.1.call-done), kind=kLoop, calls=%fused_computation.2 | loop fusion | flops 16514304 | bytes 11013120 | tf_op jit(solution)/shard_map/reduce_sum | solution.py:19
  82.9 146.4 %all-gather.9.cloned.1.call-done = bf16[7168,1024]{1,0:T(8,128)(2,1)} async-done(((bf16[896,1024]{1,0:T(8,128)(2,1)}), bf16[7168,1024]{1,0:T(8,128)(2,1)}) %all-gather.9.cloned.1.call-update) | async-done | bytes 14680080 | tf_op jit(solution)/shard_map/all_gather | solution.py:15
  229.3 18.9 %fusion.12 = (f32[384,2]{0,1:T(2,128)S(1)}, f32[384,2,1024]{2,0,1:T(8,128)S(1)}) fusion(bf16[7168,1024]{1,0:T(8,128)(2,1)} %all-gather.9.cloned.1.call-done, bf16[384,2,7168]{0,2,1:T(8,128)(2,1)} %all-gather.7.cloned.1.call-done, f32[2,7168]{1,0:T(2,128)S(1)} %bitcast.42, f32[384,2]{0,1:T(2,128)S(1)} %add_rsqrt_fusion), kind=kOutput, calls=%fused_computation.38 | convolution fusion | flops 11297094656 | bytes 28899328 | tf_op jit(solution)/shard_map/tmd,dv->tmv/dot_general | solution.py:23
  248.2 1.1 exponential_reduce_fusion
  249.3 24.8 %all-gather = f32[96,384,2]{1,2,0:T(2,128)S(1)} all-gather(f32[3,384,2]{1,2,0:T(2,128)S(1)} %pad_maximum_fusion), channel_id=2, replica_groups=mesh['row'=8,'col'=32] {'col'}, dimensions={0}, use_global_device_ids=true | all-gather | bytes 304128 | tf_op jit(solution)/shard_map/all_gather | solution.py:30
  274.1 0.1 bitcast_reduce_fusion
  274.2 0.1 fusion.9
  274.4 0.2 select_reduce_fusion.3
  274.5 23.3 %all-gather.3 = f32[8,3,16]{2,1,0:T(4,128)S(1)} all-gather(f32[1,3,16]{2,1,0:T(4,128)S(1)} %maximum_bitcast_fusion), channel_id=3, replica_groups=mesh['row'=8,'col'=32] {'row'}, dimensions={0}, use_global_device_ids=true | all-gather | bytes 1728 | tf_op jit(solution)/shard_map/all_gather | solution.py:43
  297.9 0.6 copy.25
  (12 shorter events, 0.2 us)
Async XLA Ops:
  6.5 70.0 %all-gather.7.cloned.1.call-start = ((), (), s32[]{:S(2)}) async-start(), calls=%async_computation | async-start | bytes 11354112 | tf_op jit(solution)/shard_map/all_gather | solution.py:16
  7.3 222.0 %all-gather.9.cloned.1.call-start = ((), (), s32[]{:S(2)}) async-start(), calls=%async_computation.1 | async-start | bytes 16515072 | tf_op jit(solution)/shard_map/all_gather | solution.py:15
Sparse Core Ops, SparseCore 0:
  9.9 66.5 all-gather.6
  78.3 150.8 all-gather.8
where the time goes:
time: 306 us; the launch traced here: 305 us
  waiting for transfers between devices  189 us (62%)
  blocking collectives  72.7 us (24%)
  matrix products  18.9 us (6%)
  between operations  13.5 us (4%)
  other arithmetic  9.79 us (3%)
    all_gather x1, waiting for transfers between devices, per_device(): full_unembed = lax.all_gather(unembed, 'row', axis=0, tiled=True)  146 us
    all_gather x1, waiting for transfers between devices, per_device(): full_hidden = lax.all_gather(hidden_in, 'col', axis=2, tiled=True)  41.2 us
    all_gather x1, blocking collectives, per_device(): parts = lax.all_gather(jnp.stack([row_max, exp_total, picked]), 'col')  24.8 us
    all_gather x1, blocking collectives, per_device(): full_gain = lax.all_gather(final_gain, 'col', axis=1, tiled=True)  24.5 us
    all_gather x1, blocking collectives, per_device(): stats = lax.all_gather(jnp.stack([ratio_sums, squares, ratio_max]), 'row')  23.3 us
    dot_general x1, matrix products, per_device(): jnp.einsum('tmd,dv->tmv', features, full_unembed, preferred_element_type=...  18.9 us
    reduce_sum x1, other arithmetic, per_device(): mean_square = jnp.sum(stream * stream, axis=2) / D  6.34 us
  transfers between devices with their start and end apart: 2, of which 2 were waited for; matrix products, arithmetic and copies ran while one was open for 3% of the time, Pallas kernels for 0%

commit v1 on v0

--- a/solution.py
+++ b/solution.py
@@ -7,12 +7,35 @@
 EPS = 1e-05
 
 
+def review_vector(u_in, shard_axis="row"):
+    r2 = lax.axis_size(shard_axis)
+    everything = lax.axis_index(shard_axis)
+    e_next, part_now, carry = (r2, everything, u_in.shape[0])
+    rack = [s * e_next if j0 == 0 else s for j0, s in enumerate(u_in.shape)]
+    odd = jnp.zeros(rack, u_in.dtype)
+    state_next = lax.dynamic_update_slice_in_dim(odd, u_in, part_now * carry, axis=0)
+    res = out_arr = u_in
+    for k in range(1, e_next // 2 + 1):
+        y_new = map(lambda j0: (j0, (j0 + 1) % e_next), range(e_next))
+        res = lax.ppermute(res, shard_axis, list(y_new))
+        state_next = lax.dynamic_update_slice_in_dim(
+            state_next, res, (part_now - k) % e_next * carry, axis=0
+        )
+        if 2 * k < e_next:
+            reached = map(lambda j0: (j0, (j0 - 1) % e_next), range(e_next))
+            out_arr = lax.ppermute(out_arr, shard_axis, list(reached))
+            state_next = lax.dynamic_update_slice_in_dim(
+                state_next, out_arr, (part_now + k) % e_next * carry, axis=0
+            )
+    return state_next
+
+
 def per_device(hidden_in, final_gain, unembed, lengths, targets, owner):
     tok_rows = hidden_in.shape[0]
     vocab_cols = unembed.shape[1]
     col_index = lax.axis_index("col")
     row_index = lax.axis_index("row")
-    full_unembed = lax.all_gather(unembed, "row", axis=0, tiled=True)
+    full_unembed = review_vector(unembed)
     full_hidden = lax.all_gather(hidden_in, "col", axis=2, tiled=True)
     full_gain = lax.all_gather(final_gain, "col", axis=1, tiled=True)
     stream = full_hidden.astype(jnp.float32)

time: 306 us -> 276 us (0.902)
  waiting for transfers between devices: 189 us -> 119 us
  local copies, waits for them, and re-layouts: 1.43 us -> 31.6 us
  starting transfers between devices: 0.04 us -> 9.45 us
    all_gather x1 -> x0, waiting for transfers between devices: 146 us -> none  [per_device(): full_unembed = lax.all_gather(unembed, 'row', axis=0, tiled=True)]
    ppermute x0 -> x7, waiting for transfers between devices: none -> 118 us  [the longest x4 118 us: review_vector(): res = lax.ppermute(res, shard_axis, list(y_new))]
    all_gather x1, waiting for transfers between devices: 41.2 us -> 0.01 us  [per_device(): full_hidden = lax.all_gather(hidden_in, 'col', axis=2, tiled=True)]
    dynamic_update_slice x0 -> x8, local copies, waits for them, and re-layouts: none -> 21.8 us  [the longest x4 11.6 us: review_vector(): lax.dynamic_update_slice_in_dim(state_next, res, (part_now - k) % e_next...]
    ppermute x0 -> x7, starting transfers between devices: none -> 9.45 us  [the longest x3 5.53 us: review_vector(): out_arr = lax.ppermute(out_arr, shard_axis, list(reached))]
    broadcast_in_dim x0 -> x1, local copies, waits for them, and re-layouts: none -> 7.1 us  [review_vector(): odd = jnp.zeros(rack, u_in.dtype)]
  transfers between devices with their start and end apart: 2 -> 8, of which waited for: 2 -> 3; matrix products, arithmetic and copies ran while one was open for 3% -> 11% of each run, Pallas kernels for 0% -> 0%
where the time goes in v1:
time: 276 us; the launch traced here: 275 us
  waiting for transfers between devices  119 us (43%)
  blocking collectives  74.5 us (27%)
  local copies, waits for them, and re-layouts  31.6 us (11%)
  matrix products  18.9 us (7%)
  between operations  13.5 us (5%)
  starting transfers between devices  9.45 us (3%)
  other arithmetic  8.4 us (3%)
    ppermute x4, waiting for transfers between devices, review_vector(): res = lax.ppermute(res, shard_axis, list(y_new))  118 us
    all_gather x1, blocking collectives, per_device(): stats = lax.all_gather(jnp.stack([ratio_sums, squares, ratio_max]), 'row')  25.3 us
    all_gather x1, blocking collectives, per_device(): full_gain = lax.all_gather(final_gain, 'col', axis=1, tiled=True)  24.9 us
    all_gather x1, blocking collectives, per_device(): parts = lax.all_gather(jnp.stack([row_max, exp_total, picked]), 'col')  24.2 us
    dot_general x1, matrix products, per_device(): jnp.einsum('tmd,dv->tmv', features, full_unembed, preferred_element_type=...  18.9 us
    dynamic_update_slice x4, local copies, waits for them, and re-layouts, review_vector(): lax.dynamic_update_slice_in_dim(state_next, res, (part_now - k) % e_next...  11.6 us
    dynamic_update_slice x3, local copies, waits for them, and re-layouts, review_vector(): lax.dynamic_update_slice_in_dim(state_next, out_arr, (part_now + k) % e_n...  8.79 us
    broadcast_in_dim x1, local copies, waits for them, and re-layouts, review_vector(): odd = jnp.zeros(rack, u_in.dtype)  7.1 us
  transfers between devices with their start and end apart: 8, of which 3 were waited for; matrix products, arithmetic and copies ran while one was open for 11% of the time, Pallas kernels for 0%

profile of v1, /device:TPU:32, one launch (start us, length us, event | category | flops | bytes accessed | tf_op | source)
XLA Modules:
  0.0 275.2 jit_solution(7017435977189560711)
XLA Ops:
  6.5 0.0 copy-start
  6.5 0.0 copy-start.4
  6.5 0.0 copy-start.3
  6.5 0.0 all-gather.6.cloned.1.call-start
  6.5 0.7 all-gather.6.cloned.1.call-update
  7.3 2.0 collective-permute-start
  9.3 0.1 collective-permute-start.1
  9.4 39.9 %collective-permute-done = bf16[896,1024]{1,0:T(8,128)(2,1)S(1)} collective-permute-done((bf16[896,1024]{1,0:T(8,128)(2,1)}, bf16[896,1024]{1,0:T(8,128)(2,1)S(1)}, u32[]{:S(2)}, u32[]{:S(2)}) %collective-permute-start) | collective-permute-done | bytes 1835040 | tf_op jit(solution)/shard_map/ppermute | solution.py:20
  49.3 1.3 copy-done.1
  50.6 1.9 collective-permute-start.2
  52.5 0.0 collective-permute-done.1
  52.5 2.4 collective-permute-start.3
  54.9 39.4 %collective-permute-done.2 = bf16[896,1024]{1,0:T(8,128)(2,1)} collective-permute-done((bf16[896,1024]{1,0:T(8,128)(2,1)S(1)}, bf16[896,1024]{1,0:T(8,128)(2,1)}, u32[]{:S(2)}, u32[]{:S(2)}) %collective-permute-start.2) | collective-permute-done | bytes 1835040 | tf_op jit(solution)/shard_map/ppermute | solution.py:20
  94.3 0.0 copy-done.2
  94.3 0.0 collective-permute-start.4
  94.3 0.0 collective-permute-done.3
  94.4 3.0 %collective-permute-start.5 = (bf16[896,1024]{1,0:T(8,128)(2,1)}, bf16[896,1024]{1,0:T(8,128)(2,1)}, u32[]{:S(2)}, u32[]{:S(2)}) collective-permute-start(bf16[896,1024]{1,0:T(8,128)(2,1)} %collective-permute-done.3), channel_id=1, source_target_pairs={{0,224},{32,0},{64,32},{96,64},{128,96},{160,128},{192,160},{224,1... | collective-permute-start | bytes 5505032 | tf_op jit(solution)/shard_map/ppermute | solution.py:26
  97.4 38.8 %collective-permute-done.4 = bf16[896,1024]{1,0:T(8,128)(2,1)} collective-permute-done((bf16[896,1024]{1,0:T(8,128)(2,1)}, bf16[896,1024]{1,0:T(8,128)(2,1)}, u32[]{:S(2)}, u32[]{:S(2)}) %collective-permute-start.4) | collective-permute-done | bytes 1835040 | tf_op jit(solution)/shard_map/ppermute | solution.py:20
  136.2 0.0 collective-permute-start.6
  136.2 24.9 %all-gather.2 = f32[32,224,2]{1,2,0:T(2,128)S(1)} all-gather(f32[1,224,2]{1,2,0:T(2,128)} %bitcast.49), channel_id=1, replica_groups=mesh['row'=8,'col'=32] {'col'}, dimensions={0}, use_global_device_ids=true | all-gather | bytes 59136 | tf_op jit(solution)/shard_map/all_gather | solution.py:40
  161.1 0.1 reshape.144
  161.2 0.7 copy.21
  162.0 0.1 reduce.5
  162.2 0.1 convert_reduce_fusion
  162.3 7.1 %broadcast_in_dim.71 = bf16[7168,1024]{1,0:T(8,128)(2,1)} broadcast(bf16[]{:T(256)} %constant.71.clone.1), dimensions={} | broadcast | bytes 14680066 | tf_op jit(solution)/shard_map/broadcast_in_dim | solution.py:15
  169.4 0.0 copy-done
  169.4 1.4 constant_dynamic-update-slice_fusion.7
  170.7 0.0 copy-done.4
  170.8 0.0 copy-done.3
  170.8 0.3 broadcast_compare_fusion
  171.1 2.9 %constant_dynamic-update-slice_fusion.6 = bf16[7168,1024]{1,0:T(8,128)(2,1)} fusion(bf16[7168,1024]{1,0:T(8,128)(2,1)} %constant_dynamic-update-slice_fusion.7, bf16[896,1024]{1,0:T(8,128)(2,1)} %copy-done.1, s32[]{:T(128)S(6)} %select_n.82), kind=kLoop, calls=%fused_computation.40 | loop fusion | bytes 3670020 | tf_op jit(solution)/shard_map/dynamic_update_slice | solution.py:21
  174.0 2.9 %constant_dynamic-update-slice_fusion.5 = bf16[7168,1024]{1,0:T(8,128)(2,1)} fusion(bf16[7168,1024]{1,0:T(8,128)(2,1)} %constant_dynamic-update-slice_fusion.6, bf16[896,1024]{1,0:T(8,128)(2,1)} %copy-done.2, s32[]{:T(128)S(6)} %select_n.84), kind=kLoop, calls=%fused_computation.39 | loop fusion | bytes 3670020 | tf_op jit(solution)/shard_map/dynamic_update_slice | solution.py:27
  176.8 2.9 %constant_dynamic-update-slice_fusion.4 = bf16[7168,1024]{1,0:T(8,128)(2,1)} fusion(bf16[7168,1024]{1,0:T(8,128)(2,1)} %constant_dynamic-update-slice_fusion.5, bf16[896,1024]{1,0:T(8,128)(2,1)} %collective-permute-done.2, s32[]{:T(128)S(6)} %select_n.86), kind=kLoop, calls=%fused_computation.38 | loop fusion | bytes 3670020 | tf_op jit(solution)/shard_map/dynamic_update_slice | solution.py:21
  179.8 2.9 %constant_dynamic-update-slice_fusion.3 = bf16[7168,1024]{1,0:T(8,128)(2,1)} fusion(bf16[7168,1024]{1,0:T(8,128)(2,1)} %constant_dynamic-update-slice_fusion.4, bf16[896,1024]{1,0:T(8,128)(2,1)} %collective-permute-done.3, s32[]{:T(128)S(6)} %select_n.88), kind=kLoop, calls=%fused_computation.37 | loop fusion | bytes 3670020 | tf_op jit(solution)/shard_map/dynamic_update_slice | solution.py:27
  182.7 2.9 %constant_dynamic-update-slice_fusion.2 = bf16[7168,1024]{1,0:T(8,128)(2,1)} fusion(bf16[7168,1024]{1,0:T(8,128)(2,1)} %constant_dynamic-update-slice_fusion.3, bf16[896,1024]{1,0:T(8,128)(2,1)} %collective-permute-done.4, s32[]{:T(128)S(6)} %select_n.90), kind=kLoop, calls=%fused_computation.36 | loop fusion | bytes 3670020 | tf_op jit(solution)/shard_map/dynamic_update_slice | solution.py:21
  185.6 0.0 collective-permute-done.5
  185.6 3.0 %constant_dynamic-update-slice_fusion.1 = bf16[7168,1024]{1,0:T(8,128)(2,1)} fusion(bf16[7168,1024]{1,0:T(8,128)(2,1)} %constant_dynamic-update-slice_fusion.2, bf16[896,1024]{1,0:T(8,128)(2,1)} %collective-permute-done.5, s32[]{:T(128)S(6)} %select_n.92), kind=kLoop, calls=%fused_computation.35 | loop fusion | bytes 3670020 | tf_op jit(solution)/shard_map/dynamic_update_slice | solution.py:27
  188.5 0.0 collective-permute-done.6
  188.5 2.9 %constant_dynamic-update-slice_fusion = bf16[7168,1024]{1,0:T(8,128)(2,1)} fusion(bf16[7168,1024]{1,0:T(8,128)(2,1)} %constant_dynamic-update-slice_fusion.1, bf16[896,1024]{1,0:T(8,128)(2,1)} %collective-permute-done.6, s32[]{:T(128)S(6)} %select_n.94), kind=kLoop, calls=%fused_computation.34 | loop fusion | bytes 3670020 | tf_op jit(solution)/shard_map/dynamic_update_slice | solution.py:21
  191.4 6.3 %fusion = f32[384,2]{0,1:T(2,128)S(1)} fusion(bf16[384,2,7168]{0,2,1:T(8,128)(2,1)} %all-gather.6.cloned.1.call-done), kind=kLoop, calls=%fused_computation.2 | loop fusion | flops 16514304 | bytes 11013120 | tf_op jit(solution)/shard_map/reduce_sum | solution.py:42
  197.8 18.9 %fusion.12 = (f32[384,2]{0,1:T(2,128)S(1)}, f32[384,2,1024]{2,0,1:T(8,128)S(1)}) fusion(bf16[7168,1024]{1,0:T(8,128)(2,1)} %constant_dynamic-update-slice_fusion, bf16[384,2,7168]{0,2,1:T(8,128)(2,1)} %all-gather.6.cloned.1.call-done, f32[2,7168]{1,0:T(2,128)S(1)} %bitcast.42, f32[384,2]{0,1:T(2,128)S(1)} %add_rsqrt_fusion), kind=kOutput, calls=%fused_computation.46 | convolution fusion | flops 11297094656 | bytes 28899328 | tf_op jit(solution)/shard_map/tmd,dv->tmv/dot_general | solution.py:46
  216.7 1.1 exponential_reduce_fusion
  217.8 24.2 %all-gather = f32[96,384,2]{1,2,0:T(2,128)S(1)} all-gather(f32[3,384,2]{1,2,0:T(2,128)S(1)} %pad_maximum_fusion), channel_id=2, replica_groups=mesh['row'=8,'col'=32] {'col'}, dimensions={0}, use_global_device_ids=true | all-gather | bytes 304128 | tf_op jit(solution)/shard_map/all_gather | solution.py:53
  242.0 0.1 bitcast_reduce_fusion
  242.1 0.1 fusion.9
  242.2 0.2 select_reduce_fusion.3
  242.4 25.3 %all-gather.3 = f32[8,3,16]{2,1,0:T(4,128)S(1)} all-gather(f32[1,3,16]{2,1,0:T(4,128)S(1)} %maximum_bitcast_fusion), channel_id=3, replica_groups=mesh['row'=8,'col'=32] {'row'}, dimensions={0}, use_global_device_ids=true | all-gather | bytes 1728 | tf_op jit(solution)/shard_map/all_gather | solution.py:66
  267.8 0.6 copy.25
  (16 shorter events, 0.2 us)
Async XLA Ops:
  6.5 162.8 %copy-start = (bf16[896,1024]{1,0:T(8,128)(2,1)S(1)}, bf16[896,1024]{1,0:T(8,128)(2,1)}, u32[]{:S(2)}) copy-start(bf16[896,1024]{1,0:T(8,128)(2,1)} %param.8) | copy-start | bytes 5505028
  6.5 164.2 %copy-start.4 = (s32[16]{0:T(128)S(1)}, s32[16]{0:T(128)}, u32[]{:S(2)}) copy-start(s32[16]{0:T(128)} %param.11) | copy-start | bytes 196
  6.5 164.2 %copy-start.3 = (s32[384]{0:T(512)S(1)}, s32[384]{0:T(512)}, u32[]{:S(2)}) copy-start(s32[384]{0:T(512)} %param.10) | copy-start | bytes 4612
  6.5 184.9 %all-gather.6.cloned.1.call-start = ((), (), s32[]{:S(2)}) async-start(), calls=%async_computation | async-start | bytes 11354112 | tf_op jit(solution)/shard_map/all_gather | solution.py:39
  7.3 42.0 %collective-permute-start = (bf16[896,1024]{1,0:T(8,128)(2,1)}, bf16[896,1024]{1,0:T(8,128)(2,1)S(1)}, u32[]{:S(2)}, u32[]{:S(2)}) collective-permute-start(bf16[896,1024]{1,0:T(8,128)(2,1)} %param.8), channel_id=1, source_target_pairs={{0,32},{32,64},{64,96},{96,128},{128,160},{160,192},{192,224},{224... | collective-permute-start | bytes 5505032 | tf_op jit(solution)/shard_map/ppermute | solution.py:20
  9.3 43.2 %collective-permute-start.1 = (bf16[896,1024]{1,0:T(8,128)(2,1)}, bf16[896,1024]{1,0:T(8,128)(2,1)S(1)}, u32[]{:S(2)}, u32[]{:S(2)}) collective-permute-start(bf16[896,1024]{1,0:T(8,128)(2,1)} %param.8), channel_id=1, source_target_pairs={{0,224},{32,0},{64,32},{96,64},{128,96},{160,128},{192,160},{224,1... | collective-permute-start | bytes 5505032 | tf_op jit(solution)/shard_map/ppermute | solution.py:26
  49.3 1.3 copy-start.1
  50.6 43.8 %collective-permute-start.2 = (bf16[896,1024]{1,0:T(8,128)(2,1)S(1)}, bf16[896,1024]{1,0:T(8,128)(2,1)}, u32[]{:S(2)}, u32[]{:S(2)}) collective-permute-start(bf16[896,1024]{1,0:T(8,128)(2,1)S(1)} %collective-permute-done), channel_id=1, source_target_pairs={{0,32},{32,64},{64,96},{96,128},{128,160},{160,192},{192,224},{224... | collective-permute-start | bytes 5505032 | tf_op jit(solution)/shard_map/ppermute | solution.py:20
  52.5 41.8 %copy-start.2 = (bf16[896,1024]{1,0:T(8,128)(2,1)}, bf16[896,1024]{1,0:T(8,128)(2,1)S(1)}, u32[]{:S(2)}) copy-start(bf16[896,1024]{1,0:T(8,128)(2,1)S(1)} %collective-permute-done.1) | copy-start | bytes 5505028
  52.5 41.8 %collective-permute-start.3 = (bf16[896,1024]{1,0:T(8,128)(2,1)S(1)}, bf16[896,1024]{1,0:T(8,128)(2,1)}, u32[]{:S(2)}, u32[]{:S(2)}) collective-permute-start(bf16[896,1024]{1,0:T(8,128)(2,1)S(1)} %collective-permute-done.1), channel_id=1, source_target_pairs={{0,224},{32,0},{64,32},{96,64},{128,96},{160,128},{192,160},{224,1... | collective-permute-start | bytes 5505032 | tf_op jit(solution)/shard_map/ppermute | solution.py:26
  94.3 41.8 %collective-permute-start.4 = (bf16[896,1024]{1,0:T(8,128)(2,1)}, bf16[896,1024]{1,0:T(8,128)(2,1)}, u32[]{:S(2)}, u32[]{:S(2)}) collective-permute-start(bf16[896,1024]{1,0:T(8,128)(2,1)} %collective-permute-done.2), channel_id=1, source_target_pairs={{0,32},{32,64},{64,96},{96,128},{128,160},{160,192},{192,224},{224... | collective-permute-start | bytes 5505032 | tf_op jit(solution)/shard_map/ppermute | solution.py:20
  94.4 91.2 %collective-permute-start.5 = (bf16[896,1024]{1,0:T(8,128)(2,1)}, bf16[896,1024]{1,0:T(8,128)(2,1)}, u32[]{:S(2)}, u32[]{:S(2)}) collective-permute-start(bf16[896,1024]{1,0:T(8,128)(2,1)} %collective-permute-done.3), channel_id=1, source_target_pairs={{0,224},{32,0},{64,32},{96,64},{128,96},{160,128},{192,160},{224,1... | collective-permute-start | bytes 5505032 | tf_op jit(solution)/shard_map/ppermute | solution.py:26
  136.2 52.4 %collective-permute-start.6 = (bf16[896,1024]{1,0:T(8,128)(2,1)}, bf16[896,1024]{1,0:T(8,128)(2,1)}, u32[]{:S(2)}, u32[]{:S(2)}) collective-permute-start(bf16[896,1024]{1,0:T(8,128)(2,1)} %collective-permute-done.4), channel_id=1, source_target_pairs={{0,32},{32,64},{64,96},{96,128},{128,160},{160,192},{192,224},{224... | collective-permute-start | bytes 5505032 | tf_op jit(solution)/shard_map/ppermute | solution.py:20
Sparse Core Ops, SparseCore 0:
  9.9 66.4 all-gather.5
